TPU v7x, 32 devices: a whole 2x2x4 slice. The times are simulated.
32 devices in a mesh: shot: 4 (over y, core), tile: 8 (over z, x).
Axes of the slice: x: 2, y: 2, z: 4, core: 2. Of those that a mesh axis runs over, the one named last changes fastest.
Arguments:
- coefs: float32 [3, 16, 1024, 128], P(None, 'shot', 'tile')
- fwd_state: float32 [4, 4, 16, 1024, 128], P('shot', None, None, 'tile'), may hold values from -3 to 3
- adj_state: float32 [4, 4, 16, 1024, 128], P('shot', None, None, 'tile'), may hold values from -3 to 3
- src_cell: int32 [4, 8], P('shot', 'tile'), may hold values from 0 to 262143
- src_wave: float32 [4, 6], P('shot'), may hold values from -8 to 8
- rec_cells: int32 [4, 1024], P('shot', 'tile'), may hold values from 0 to 262143
- observed: float32 [4, 6, 1024], P('shot', None, 'tile'), may hold values from -6 to 6
Outputs:
- gradient: float32 [3, 16, 1024, 128], P(None, 'shot', 'tile')
- fwd_final: float32 [4, 2, 16, 1024, 128], P('shot', None, None, 'tile')
- adj_final: float32 [4, 2, 16, 1024, 128], P('shot', None, None, 'tile')
Inputs may be any that keep to these rules, and one draw needn't show every extreme that they name: `src_cell`: local cell index depth * 128 * 128 + first * 128 + second inside the aperture tile. `rec_cells`: local cell index inside the tile of the receiver's block; cells may repeat.
All inputs are finite; a program needn't handle non-finite values.
Results may differ from a plain program's by a relative error of at most 0.0003.
Values sent between devices are 32-bit elements; how exact they have to be, the bound alone decides.
No kernel may reach another device: no remote copies, remote signals or barrier semaphores. Data moves between devices by JAX's collectives and lax.ppermute only.
A program may use at most 192 MiB of HBM per device.

v0:
```python
import jax
import jax.numpy as jnp
from jax import lax
from jax.sharding import PartitionSpec as P

HALO = 12


def taps(padded, size, axis):

    def part(k):
        return lax.slice_in_dim(padded, k, k + size, axis=axis)

    return (-part(0) + 16.0 * part(1) - 30.0 * part(2) + 16.0 * part(3) - part(4)) / 12.0


def along_local(field, axis):
    pads = [(0, 0)] * field.ndim
    pads[axis] = (2, 2)
    return taps(jnp.pad(field, pads), field.shape[axis], axis)


def horiz(field):
    return along_local(field, field.ndim - 2) + along_local(field, field.ndim - 1)


def to_left_right(head, tail, axis):
    count = lax.axis_size(axis)
    from_left = lax.ppermute(tail, axis, [(i, i + 1) for i in range(count - 1)])
    from_right = lax.ppermute(head, axis, [(i + 1, i) for i in range(count - 1)])
    return (from_left, from_right)


def rows(x):
    return x.reshape(-1, x.shape[-1])


def per_device(coefs, fwd_state, adj_state, src_cell, src_wave, rec_cells, observed):
    w = HALO
    _, zl, ax, ay = coefs.shape
    n_tile = lax.axis_size("tile")
    tile = lax.axis_index("tile")
    steps = src_wave.shape[1]
    full = lax.all_gather(coefs, "shot", axis=1, tiled=True)
    az = full.shape[1]
    xe = ax + 2 * w
    ext_shape = (az, xe, ay)
    cells_ext = az * xe * ay
    fs = fwd_state[0]
    src_row = jnp.broadcast_to(src_cell[0, 0].astype(jnp.float32), (1, ay))
    head1 = jnp.concatenate([rows(fs[:, :, :w]), rows(coefs[:, :, :w]), src_row], axis=0)
    tail1 = jnp.concatenate(
        [rows(fs[:, :, ax - w :]), rows(coefs[:, :, ax - w :]), src_row], axis=0
    )
    left1, right1 = to_left_right(head1, tail1, "tile")
    n_fs = 4 * az * w
    n_cf = 3 * zl * w

    def unpack1(m):
        st = m[:n_fs].reshape(4, az, w, ay)
        cf = m[n_fs : n_fs + n_cf].reshape(3, zl, w, ay)
        sc = m[n_fs + n_cf, 0]
        return (st, cf, sc)

    st_l, cf_l, sc_l = unpack1(left1)
    st_r, cf_r, sc_r = unpack1(right1)
    cf_halo = lax.all_gather(jnp.concatenate([cf_l, cf_r], axis=2), "shot", axis=1, tiled=True)
    full_ext = jnp.concatenate([cf_halo[:, :, :w], full, cf_halo[:, :, w:]], axis=2)
    speed, stretch, couple = (full_ext[0], full_ext[1], full_ext[2])
    state = jnp.concatenate([st_l, fs, st_r], axis=2)
    ad = adj_state[0]
    left2, right2 = to_left_right(rows(ad[:, :, :w]), rows(ad[:, :, ax - w :]), "tile")
    adj_ext = jnp.concatenate(
        [left2.reshape(4, az, w, ay), ad, right2.reshape(4, az, w, ay)], axis=2
    )

    def ext_index(cell, shift):
        depth = cell // (ax * ay)
        first = cell // ay % ax + shift + w
        second = cell % ay
        ok = (first >= 0) & (first < xe)
        return (jnp.where(ok, (depth * xe + first) * ay + second, cells_ext), ok)

    src_own, _ = ext_index(src_cell[0, 0], 0)
    src_lft, ok_l = ext_index(sc_l.astype(jnp.int32), -ax)
    src_rgt, ok_r = ext_index(sc_r.astype(jnp.int32), ax)
    ok_l = ok_l & (tile > 0)
    ok_r = ok_r & (tile < n_tile - 1)
    src_idx = jnp.stack([src_own, src_lft, src_rgt])
    src_on = jnp.stack([jnp.float32(1.0), ok_l.astype(jnp.float32), ok_r.astype(jnp.float32)])
    source_mask = (
        jnp.zeros((cells_ext,), jnp.float32).at[src_idx].add(src_on, mode="drop").reshape(ext_shape)
    )
    receivers = rec_cells[0]
    rec_own, _ = ext_index(receivers, 0)
    upper, lower, upper_old, lower_old = (state[0], state[1], state[2], state[3])
    stored = []
    records = []
    for step in range(steps):
        h = horiz(upper)
        z = along_local(lower, 0)
        pulse = src_wave[0, step] * source_mask
        upper_next = 2.0 * upper - upper_old + speed * (stretch * h + couple * z) + pulse
        lower_next = 2.0 * lower - lower_old + speed * (couple * h + z) + pulse
        stored.append((h[:, w : w + ax], z[:, w : w + ax]))
        records.append(upper_next.reshape(-1)[rec_own] - observed[0, step])
        upper_old, lower_old, upper, lower = (upper, lower, upper_next, lower_next)
    msg = jnp.concatenate([jnp.stack(records), receivers.astype(jnp.float32)[None]], axis=0)
    left3, right3 = to_left_right(msg, msg, "tile")
    rec_l, okr_l = ext_index(left3[steps].astype(jnp.int32), -ax)
    rec_r, okr_r = ext_index(right3[steps].astype(jnp.int32), ax)
    okr_l = okr_l & (tile > 0)
    okr_r = okr_r & (tile < n_tile - 1)
    rec_l = jnp.where(okr_l, rec_l, cells_ext)
    rec_r = jnp.where(okr_r, rec_r, cells_ext)
    rec_all = jnp.concatenate([rec_own, rec_l, rec_r])
    lam, mu, lam_old, mu_old = (adj_ext[0], adj_ext[1], adj_ext[2], adj_ext[3])
    acc_h = jnp.zeros((az, ax, ay), jnp.float32)
    acc_x = jnp.zeros((az, ax, ay), jnp.float32)
    acc_z = jnp.zeros((az, ax, ay), jnp.float32)
    for step in reversed(range(steps)):
        first = speed * (stretch * lam + couple * mu)
        other = speed * (couple * lam + mu)
        vals = jnp.concatenate([records[step], left3[step], right3[step]])
        inject = (
            jnp.zeros((cells_ext,), jnp.float32)
            .at[rec_all]
            .add(vals, mode="drop")
            .reshape(ext_shape)
        )
        lam_new = inject + 2.0 * lam + horiz(first) - lam_old
        mu_new = 2.0 * mu + along_local(other, 0) - mu_old
        h, z = stored[step]
        ln = lam_new[:, w : w + ax]
        mn = mu_new[:, w : w + ax]
        acc_h = acc_h + ln * h
        acc_x = acc_x + ln * z + mn * h
        acc_z = acc_z + mn * z
        lam_old, mu_old, lam, mu = (lam, mu, lam_new, mu_new)
    n_shot = lax.axis_size("shot")
    acc = jnp.stack([acc_h, acc_x, acc_z])
    acc = acc.reshape(3, n_shot, az // n_shot, ax, ay).transpose(1, 0, 2, 3, 4)
    summed = lax.psum_scatter(acc, "shot", scatter_dimension=0, tiled=True)[0]
    q_h, q_x, q_z = (summed[0], summed[1], summed[2])
    c, a, b = (coefs[0], coefs[1], coefs[2])
    gradient = jnp.stack([a * q_h + b * q_x + q_z, c * q_h, c * q_x])
    fwd_final = jnp.stack([upper[:, w : w + ax], lower[:, w : w + ax]])[None]
    adj_final = jnp.stack([lam[:, w : w + ax], mu[:, w : w + ax]])[None]
    return (gradient, fwd_final, adj_final)


def solution(mesh):
    placed = (
        P(None, "shot", "tile", None),
        P("shot", None, None, "tile", None),
        P("shot", None, None, "tile", None),
        P("shot", "tile"),
        P("shot", None),
        P("shot", "tile"),
        P("shot", None, "tile"),
    )
    return jax.shard_map(
        per_device,
        mesh=mesh,
        in_specs=placed,
        out_specs=(
            P(None, "shot", "tile", None),
            P("shot", None, None, "tile", None),
            P("shot", None, None, "tile", None),
        ),
        check_vma=False,
    )
```

profile of v0, /device:TPU:0, one launch (start us, length us, event | category | flops | bytes accessed | tf_op | source)
XLA Modules:
  0.0 317.3 jit_solution(9708239038787714301)
XLA Ops:
  12.6 5.5 %collective-permute-start = (f32[913,128]{1,0:T(8,128)S(1)}, f32[913,128]{1,0:T(8,128)S(1)}, u32[]{:S(2)}, u32[]{:S(2)}) collective-permute-start(f32[913,128]{1,0:T(8,128)S(1)} %get-tuple-element.91), channel_id=1, source_target_pairs={{0,1},{1,2},{2,3},{3,4},{4,5},{5,6},{6,7},{8,9},{9,10},{10,11},{11... | collective-permute-start | bytes 1402376 | tf_op jit(solution)/shard_map/ppermute | solution.py:29
  21.6 6.2 %collective-permute-start.4 = (f32[768,128]{1,0:T(8,128)}, f32[768,128]{1,0:T(8,128)}, u32[]{:S(2)}, u32[]{:S(2)}) collective-permute-start(f32[768,128]{1,0:T(8,128)} %reshape.631), channel_id=1, source_target_pairs={{0,1},{1,2},{2,3},{3,4},{4,5},{5,6},{6,7},{8,9},{9,10},{10,11},{11... | collective-permute-start | bytes 1179656 | tf_op jit(solution)/shard_map/ppermute | solution.py:29
  28.7 6.7 %collective-permute-done.5 = f32[768,128]{1,0:T(8,128)S(1)} collective-permute-done((f32[768,128]{1,0:T(8,128)S(1)}, f32[768,128]{1,0:T(8,128)S(1)}, u32[]{:S(2)}, u32[]{:S(2)}) %collective-permute-start.5) | collective-permute-done | bytes 393248 | tf_op jit(solution)/shard_map/ppermute | solution.py:30
  35.4 18.7 %collective-permute-done.4 = f32[768,128]{1,0:T(8,128)} collective-permute-done((f32[768,128]{1,0:T(8,128)}, f32[768,128]{1,0:T(8,128)}, u32[]{:S(2)}, u32[]{:S(2)}) %collective-permute-start.4) | collective-permute-done | bytes 393248 | tf_op jit(solution)/shard_map/ppermute | solution.py:29
  57.9 7.6 %all_gather.6 = f32[3,16,24,128]{3,2,1,0:T(8,128)S(1)} all-gather(f32[3,4,24,128]{3,2,1,0:T(8,128)S(1)} %pad_maximum_fusion.4), channel_id=1, replica_groups=mesh['shot'=4,'tile'=8] {'shot'}, dimensions={1}, use_global_device_ids=true | all-gather | bytes 737280 | tf_op jit(solution)/shard_map/all_gather | solution.py:67
  67.6 5.5 %pad_maximum_fusion = (f32[4,16,152,128]{3,2,1,0:T(8,128)S(1)}, f32[4,16,152,128]{3,2,1,0:T(8,128)}) fusion(f32[4,16,12,128]{3,2,1,0:T(8,128)S(1)} %reshape.621, f32[4,16,128,128]{3,2,1,0:T(8,128)} %bitcast.466, f32[4,16,12,128]{3,2,1,0:T(8,128)S(1)} %reshape.618, f32[4,16,12,128]{3,2,1,0:T(8,128)S(1)} %reshape.634, f32[4,16,128,128]{3,2,1,0:T(8,128)} %bitcast.468, ...), kind=kLoop, calls=%fused_computation.13 | loop fusion | flops 4980736 | bytes 19922944 | tf_op jit(solution)/shard_map/concatenate | solution.py:70
  78.5 7.6 %broadcast_multiply_fusion = (f32[311296]{0:T(1024)}, f32[311296]{0:T(1024)}, f32[311296]{0:T(1024)}, f32[311296]{0:T(1024)}, f32[311296]{0:T(1024)S(1)}, /*index=5*/f32[311296]{0:T(1024)S(1)}) fusion(f32[311296]{0:T(1024)} %scatter_custom_fusion, f32[]{:T(128)} %bitcast.46, f32[]{:T(128)} %bitcast.41, f32[]{:T(128)} %bitcast.36, f32[]{:T(128)} %bitcast.31, ...), kind=kLoop, calls=%fused_computation.422 | loop fusion | flops 1867776 | bytes 8716312 | tf_op jit(solution)/shard_map/mul | solution.py:102
  86.1 2.7 pad_maximum_fusion.2
  93.1 5.0 %add_multiply_fusion.10 = (f32[16,152,128]{2,1,0:T(8,128)}, f32[16,152,128]{2,1,0:T(8,128)}, f32[16,152,128]{2,1,0:T(8,128)S(1)}, f32[16,152,128]{2,1,0:T(8,128)S(1)}, f32[16,152,128]{2,1,0:T(8,128)S(1)}) fusion(f32[4,16,152,128]{3,2,1,0:T(8,128)} %get-tuple-element.112, f32[3,16,152,128]{3,2,1,0:T(8,128)S(1)} %pad_maximum_fusion.2, ...), kind=kLoop, calls=%fused_computation.367 | loop fusion | flops 12451840 | bytes 18677760 | tf_op jit(solution)/shard_map/mul | solution.py:123
  104.1 3.0 add_add_fusion.5
  108.5 6.6 %add_add_fusion.3 = (f32[16,152,128]{2,1,0:T(8,128)}, f32[16,152,128]{2,1,0:T(8,128)}, f32[16,152,128]{2,1,0:T(8,128)}) fusion(f32[16,152,128]{2,1,0:T(8,128)S(1)} %bitcast.451, f32[16,152,128]{2,1,0:T(8,128)S(1)} %get-tuple-element.36, f32[16,152,128]{2,1,0:T(8,128)S(1)} %bitcast.433, f32[16,152,128]{2,1,0:T(8,128)S(1)} %get-tuple-element.35, ...), kind=kLoop, calls=%fused_computation.376 | loop fusion | flops 12451840 | bytes 16187392 | tf_op jit(solution)/shard_map/add | solution.py:104
  115.0 4.4 %add_add_fusion.4 = f32[16,152,128]{2,1,0:T(8,128)} fusion(f32[16,152,128]{2,1,0:T(8,128)} %bitcast.447, f32[16,152,128]{2,1,0:T(8,128)} %get-tuple-element.32, f32[16,152,128]{2,1,0:T(8,128)} %get-tuple-element.31, f32[3,16,152,128]{3,2,1,0:T(8,128)S(1)} %pad_maximum_fusion.2, f32[16,152,128]{2,1,0:T(8,128)S(1)} %bitcast.434, ...), kind=kLoop, calls=%fused_computation.379 | loop fusion | flops 7471104 | bytes 18677760 | tf_op jit(solution)/shard_map/add | solution.py:103
  119.4 12.8 %add_add_fusion.1 = (f32[16,152,128]{2,1,0:T(8,128)}, f32[16,152,128]{2,1,0:T(8,128)}, f32[16,152,128]{2,1,0:T(8,128)}) fusion(f32[16,152,128]{2,1,0:T(8,128)} %bitcast.452, f32[16,152,128]{2,1,0:T(8,128)} %bitcast.448, f32[16,152,128]{2,1,0:T(8,128)} %get-tuple-element.32, f32[16,152,128]{2,1,0:T(8,128)} %get-tuple-element.31, ...), kind=kLoop, calls=%fused_computation.372 | loop fusion | flops 14630912 | bytes 19922944 | tf_op jit(solution)/shard_map/add | solution.py:104
  132.2 6.8 %add_add_fusion.2 = f32[16,152,128]{2,1,0:T(8,128)} fusion(f32[16,152,128]{2,1,0:T(8,128)} %bitcast.453, f32[16,152,128]{2,1,0:T(8,128)} %get-tuple-element.29, f32[16,152,128]{2,1,0:T(8,128)} %get-tuple-element.28, f32[3,16,152,128]{3,2,1,0:T(8,128)S(1)} %pad_maximum_fusion.2, f32[16,152,128]{2,1,0:T(8,128)} %bitcast.449, ...), kind=kLoop, calls=%fused_computation.375 | loop fusion | flops 9961472 | bytes 22413312 | tf_op jit(solution)/shard_map/add | solution.py:103
  139.0 16.0 %add_add_fusion = (f32[16,152,128]{2,1,0:T(8,128)}, f32[16,152,128]{2,1,0:T(8,128)}, f32[16,152,128]{2,1,0:T(8,128)}) fusion(f32[16,152,128]{2,1,0:T(8,128)} %bitcast.457, f32[16,152,128]{2,1,0:T(8,128)} %bitcast.454, f32[16,152,128]{2,1,0:T(8,128)} %get-tuple-element.29, f32[16,152,128]{2,1,0:T(8,128)} %get-tuple-element.28, ...), kind=kLoop, calls=%fused_computation.371 | loop fusion | flops 20545536 | bytes 28639232 | tf_op jit(solution)/shard_map/add | solution.py:103
  168.5 5.0 %collective-permute-start.2 = (f32[7,128]{1,0:T(8,128)S(1)}, f32[7,128]{1,0:T(8,128)S(1)}, u32[]{:S(2)}, u32[]{:S(2)}) collective-permute-start(f32[7,128]{1,0:T(8,128)S(1)} %concatenate.93), channel_id=1, source_target_pairs={{0,1},{1,2},{2,3},{3,4},{4,5},{5,6},{6,7},{8,9},{9,10},{10,11},{11... | collective-permute-start | bytes 10760 | tf_op jit(solution)/shard_map/ppermute | solution.py:29
  174.9 4.4 %scatter_custom_fusion.1 = f32[311296]{0:T(1024)} fusion(s32[384]{0:T(512)S(1)} %fusion.260, f32[384]{0:T(512)S(1)} %pad_maximum_fusion.5, f32[]{:T(128)} %constant.225.clone.1), kind=kCustom, calls=%fused_computation.439 | custom fusion | flops 384 | bytes 1245188 | tf_op jit(solution)/shard_map/scatter-add | solution.py:128
  179.3 4.3 %scatter_custom_fusion.2 = f32[311296]{0:T(1024)} fusion(s32[384]{0:T(512)S(1)} %fusion.260, f32[384]{0:T(512)S(1)} %pad_maximum_fusion.6, f32[]{:T(128)} %constant.225.clone.1), kind=kCustom, calls=%fused_computation.437 | custom fusion | flops 384 | bytes 1245188 | tf_op jit(solution)/shard_map/scatter-add | solution.py:128
  183.6 4.4 %scatter_custom_fusion.3 = f32[311296]{0:T(1024)} fusion(s32[384]{0:T(512)S(1)} %fusion.260, f32[384]{0:T(512)S(1)} %pad_maximum_fusion.7, f32[]{:T(128)} %constant.225.clone.1), kind=kCustom, calls=%fused_computation.435 | custom fusion | flops 384 | bytes 1245188 | tf_op jit(solution)/shard_map/scatter-add | solution.py:128
  188.0 4.4 %scatter_custom_fusion.4 = f32[311296]{0:T(1024)} fusion(s32[384]{0:T(512)S(1)} %fusion.260, f32[384]{0:T(512)S(1)} %pad_maximum_fusion.8, f32[]{:T(128)} %constant.225.clone.1), kind=kCustom, calls=%fused_computation.433 | custom fusion | flops 384 | bytes 1245188 | tf_op jit(solution)/shard_map/scatter-add | solution.py:128
  192.4 4.6 %scatter_custom_fusion.5 = f32[311296]{0:T(1024)} fusion(s32[384]{0:T(512)S(1)} %fusion.260, f32[384]{0:T(512)S(1)} %pad_maximum_fusion.9, f32[]{:T(128)} %constant.225.clone.1), kind=kCustom, calls=%fused_computation.431 | custom fusion | flops 384 | bytes 1245188 | tf_op jit(solution)/shard_map/scatter-add | solution.py:128
  197.0 11.9 %add_multiply_fusion.9 = (f32[16,152,128]{2,1,0:T(8,128)S(1)}, f32[16,152,128]{2,1,0:T(8,128)S(1)}, f32[16,152,128]{2,1,0:T(8,128)S(1)}) fusion(f32[3,16,152,128]{3,2,1,0:T(8,128)} %copy-done, f32[4,16,152,128]{3,2,1,0:T(8,128)} %get-tuple-element.112, f32[16,152,128]{2,1,0:T(8,128)} %get-tuple-element.43, f32[16,152,128]{2,1,0:T(8,128)} %bitcast.474, ...), kind=kLoop, calls=%fused_computation.366 | loop fusion | flops 11517952 | bytes 16187392 | tf_op jit(solution)/shard_map/mul | solution.py:122
  211.1 3.7 %add_multiply_fusion.7 = (f32[16,152,128]{2,1,0:T(8,128)S(1)}, f32[16,152,128]{2,1,0:T(8,128)S(1)}, f32[16,152,128]{2,1,0:T(8,128)S(1)}) fusion(f32[3,16,152,128]{3,2,1,0:T(8,128)S(1)} %copy-done.1, f32[4,16,152,128]{3,2,1,0:T(8,128)} %get-tuple-element.112, f32[16,152,128]{2,1,0:T(8,128)S(1)} %get-tuple-element.21, f32[16,152,128]{2,1,0:T(8,128)S(1)} %bitcast.473, ...), kind=kLoop, calls=%fused_computation.362 | loop fusion | flops 11517952 | bytes 16187392 | tf_op jit(solution)/shard_map/mul | solution.py:122
  217.0 2.4 add_multiply_fusion.5
  226.2 3.4 %add_multiply_fusion.1 = (f32[16,152,128]{2,1,0:T(8,128)S(1)}, f32[16,152,128]{2,1,0:T(8,128)}, f32[16,152,128]{2,1,0:T(8,128)}) fusion(f32[3,16,152,128]{3,2,1,0:T(8,128)S(1)} %copy-done.1, f32[16,152,128]{2,1,0:T(8,128)S(1)} %get-tuple-element.16, f32[16,152,128]{2,1,0:T(8,128)S(1)} %get-tuple-element.12, f32[16,152,128]{2,1,0:T(8,128)S(1)} %bitcast.470, ...), kind=kLoop, calls=%fused_computation.350 | loop fusion | flops 11517952 | bytes 16187392 | tf_op jit(solution)/shard_map/mul | solution.py:122
  229.7 4.2 %add_subtract_fusion = (f32[16,152,128]{2,1,0:T(8,128)}, f32[16,152,128]{2,1,0:T(8,128)}, f32[16,152,128]{2,1,0:T(8,128)}, f32[16,152,128]{2,1,0:T(8,128)}, f32[16,152,128]{2,1,0:T(8,128)}, /*index=5*/f32[16,152,128]{2,1,0:T(8,128)}) fusion(f32[16,152,128]{2,1,0:T(8,128)S(1)} %get-tuple-element.7), kind=kLoop, calls=%fused_computation.349 | loop fusion | flops 3424256 | bytes 8716288 | tf_op jit(solution)/shard_map/sub | solution.py:14
  233.9 4.7 %scatter_custom_fusion.6 = f32[311296]{0:T(1024)} fusion(s32[384]{0:T(512)S(1)} %fusion.260, f32[384]{0:T(512)S(1)} %pad_maximum_fusion.10, f32[]{:T(128)} %constant.225.clone.1), kind=kCustom, calls=%fused_computation.429 | custom fusion | flops 384 | bytes 1245188 | tf_op jit(solution)/shard_map/scatter-add | solution.py:128
  238.7 3.9 %broadcast_multiply_fusion.6 = (f32[16,152,128]{2,1,0:T(8,128)}, f32[16,152,128]{2,1,0:T(8,128)S(1)}) fusion(f32[16,152,128]{2,1,0:T(8,128)} %get-tuple-element.9, f32[16,152,128]{2,1,0:T(8,128)} %get-tuple-element.8, f32[3,16,152,128]{3,2,1,0:T(8,128)} %copy-done), kind=kLoop, calls=%fused_computation.428 | loop fusion | flops 1245184 | bytes 7471104 | tf_op jit(solution)/shard_map/mul | solution.py:14
  246.7 5.2 %multiply_add_fusion.2 = (f32[16,128,128]{2,1,0:T(8,128)}, f32[16,128,128]{2,1,0:T(8,128)S(1)}) fusion(f32[16,152,128]{2,1,0:T(8,128)S(1)} %copy-done.37, f32[16,152,128]{2,1,0:T(8,128)S(1)} %copy-done.7, f32[16,152,128]{2,1,0:T(8,128)S(1)} %get-tuple-element.34, f32[16,152,128]{2,1,0:T(8,128)S(1)} %copy-done.12, f32[16,152,128]{2,1,0:T(8,128)S(1)} %copy-done.25, ...), kind=kLoop, calls=%fused_computation.420 | loop fusion | flops 5505024 | bytes 20971520 | tf_op jit(solution)/shard_map/add | solution.py:136
  253.2 6.5 %multiply_add_fusion.1 = (f32[16,128,128]{2,1,0:T(8,128)}, f32[16,128,128]{2,1,0:T(8,128)}) fusion(f32[16,128,128]{2,1,0:T(8,128)S(1)} %get-tuple-element.4, f32[16,152,128]{2,1,0:T(8,128)S(1)} %copy-done.35, f32[16,152,128]{2,1,0:T(8,128)S(1)} %copy-done.5, f32[16,152,128]{2,1,0:T(8,128)S(1)} %get-tuple-element.35, f32[16,152,128]{2,1,0:T(8,128)S(1)} %copy-done.19, ...), kind=kLoop, calls=%fused_computation.419 | loop fusion | flops 8126464 | bytes 30408704 | tf_op jit(solution)/shard_map/add | solution.py:137
  259.8 5.0 %fusion.232 = (f32[1,16,128,128]{3,2,1,0:T(8,128)S(1)}, f32[16,128,128]{2,1,0:T(8,128)S(1)}) fusion(f32[16,152,128]{2,1,0:T(8,128)} %bitcast.458, f32[16,152,128]{2,1,0:T(8,128)} %get-tuple-element.51, f32[16,152,128]{2,1,0:T(8,128)} %get-tuple-element.30, f32[16,152,128]{2,1,0:T(8,128)} %get-tuple-element.27, f32[16,152,128]{2,1,0:T(8,128)} %get-tuple-element.50, ...), kind=kLoop, calls=%fused_computation.394 | loop fusion | flops 4718592 | bytes 20971520 | tf_op jit(solution)/shard_map/stack | solution.py:147
  271.3 36.7 %reduce-scatter.2.cloned.1.call-done = f32[1,3,4,128,128]{4,3,2,1,0:T(8,128)} async-done(((f32[4,3,4,128,128]{4,3,2,1,0:T(8,128)}), f32[1,3,4,128,128]{4,3,2,1,0:T(8,128)}) %reduce-scatter.2.cloned.1.call-update) | async-done | bytes 786448 | tf_op jit(solution)/shard_map/reduce_scatter | solution.py:143
  (206 shorter events, 69.9 us)
Async XLA Ops:
  7.2 79.0 %all-gather.2.cloned.1.call-start = ((), (), s32[]{:S(2)}) async-start(), calls=%async_computation.1 | async-start | bytes 3932160 | tf_op jit(solution)/shard_map/all_gather | solution.py:44
  7.9 300.1 %reduce-scatter.2.cloned.1.call-start = ((), (), s32[]{:S(2)}) async-start(), calls=%async_computation.2 | async-start | bytes 3932160 | tf_op jit(solution)/shard_map/reduce_scatter | solution.py:143
  11.3 43.9 %collective-permute-start.1 = (f32[913,128]{1,0:T(8,128)S(1)}, f32[913,128]{1,0:T(8,128)S(1)}, u32[]{:S(2)}, u32[]{:S(2)}) collective-permute-start(f32[913,128]{1,0:T(8,128)S(1)} %get-tuple-element.92), channel_id=1, source_target_pairs={{1,0},{2,1},{3,2},{4,3},{5,4},{6,5},{7,6},{9,8},{10,9},{11,10},{12... | collective-permute-start | bytes 1402376 | tf_op jit(solution)/shard_map/ppermute | solution.py:30
  12.6 43.9 %collective-permute-start = (f32[913,128]{1,0:T(8,128)S(1)}, f32[913,128]{1,0:T(8,128)S(1)}, u32[]{:S(2)}, u32[]{:S(2)}) collective-permute-start(f32[913,128]{1,0:T(8,128)S(1)} %get-tuple-element.91), channel_id=1, source_target_pairs={{0,1},{1,2},{2,3},{3,4},{4,5},{5,6},{6,7},{8,9},{9,10},{10,11},{11... | collective-permute-start | bytes 1402376 | tf_op jit(solution)/shard_map/ppermute | solution.py:29
  19.5 8.3 %copy-start.58 = (s32[1,128]{1,0:T(1,128)S(1)}, s32[1,128]{1,0:T(1,128)}, u32[]{:S(2)}) copy-start(s32[1,128]{1,0:T(1,128)} %param.12) | copy-start | bytes 1540
  19.5 8.5 %copy-start.56 = (f32[1,6]{1,0:T(1,128)S(1)}, f32[1,6]{1,0:T(1,128)}, u32[]{:S(2)}) copy-start(f32[1,6]{1,0:T(1,128)} %param.11) | copy-start | bytes 76
  19.6 15.8 %collective-permute-start.5 = (f32[768,128]{1,0:T(8,128)S(1)}, f32[768,128]{1,0:T(8,128)S(1)}, u32[]{:S(2)}, u32[]{:S(2)}) collective-permute-start(f32[768,128]{1,0:T(8,128)S(1)} %reshape.633), channel_id=1, source_target_pairs={{1,0},{2,1},{3,2},{4,3},{5,4},{6,5},{7,6},{9,8},{10,9},{11,10},{12... | collective-permute-start | bytes 1179656 | tf_op jit(solution)/shard_map/ppermute | solution.py:30
  21.6 32.5 %collective-permute-start.4 = (f32[768,128]{1,0:T(8,128)}, f32[768,128]{1,0:T(8,128)}, u32[]{:S(2)}, u32[]{:S(2)}) collective-permute-start(f32[768,128]{1,0:T(8,128)} %reshape.631), channel_id=1, source_target_pairs={{0,1},{1,2},{2,3},{3,4},{4,5},{5,6},{6,7},{8,9},{9,10},{10,11},{11... | collective-permute-start | bytes 1179656 | tf_op jit(solution)/shard_map/ppermute | solution.py:29
  86.1 15.7 %copy-start.9 = (f32[311296]{0:T(1024)}, f32[311296]{0:T(1024)S(1)}, u32[]{:S(2)}) copy-start(f32[311296]{0:T(1024)S(1)} %get-tuple-element.73) | copy-start | bytes 3735556
  88.8 50.2 %copy-start = (f32[3,16,152,128]{3,2,1,0:T(8,128)}, f32[3,16,152,128]{3,2,1,0:T(8,128)S(1)}, u32[]{:S(2)}) copy-start(f32[3,16,152,128]{3,2,1,0:T(8,128)S(1)} %pad_maximum_fusion.2) | copy-start | bytes 11206660
  98.1 10.0 %copy-start.26 = (f32[16,152,128]{2,1,0:T(8,128)}, f32[16,152,128]{2,1,0:T(8,128)S(1)}, u32[]{:S(2)}) copy-start(f32[16,152,128]{2,1,0:T(8,128)S(1)} %get-tuple-element.52) | copy-start | bytes 3735556
  99.6 15.5 %copy-start.8 = (f32[16,152,128]{2,1,0:T(8,128)}, f32[16,152,128]{2,1,0:T(8,128)S(1)}, u32[]{:S(2)}) copy-start(f32[16,152,128]{2,1,0:T(8,128)S(1)} %fusion.220) | copy-start | bytes 3735556
  101.8 6.3 %copy-start.33 = (f32[16,152,128]{2,1,0:T(8,128)}, f32[16,152,128]{2,1,0:T(8,128)S(1)}, u32[]{:S(2)}) copy-start(f32[16,152,128]{2,1,0:T(8,128)S(1)} %get-tuple-element.36) | copy-start | bytes 3735556
  101.9 37.2 %copy-start.4 = (f32[16,152,128]{2,1,0:T(8,128)}, f32[16,152,128]{2,1,0:T(8,128)S(1)}, u32[]{:S(2)}) copy-start(f32[16,152,128]{2,1,0:T(8,128)S(1)} %get-tuple-element.38) | copy-start | bytes 3735556
  101.9 37.2 %copy-start.6 = (f32[16,152,128]{2,1,0:T(8,128)}, f32[16,152,128]{2,1,0:T(8,128)S(1)}, u32[]{:S(2)}) copy-start(f32[16,152,128]{2,1,0:T(8,128)S(1)} %get-tuple-element.37) | copy-start | bytes 3735556
  108.1 6.9 %copy-start.41 = (f32[16,152,128]{2,1,0:T(8,128)}, f32[16,152,128]{2,1,0:T(8,128)S(1)}, u32[]{:S(2)}) copy-start(f32[16,152,128]{2,1,0:T(8,128)S(1)} %add_add_fusion.6) | copy-start | bytes 3735556
  157.2 10.0 %copy-start.57 = (f32[1,6,128]{2,0,1:T(1,128)S(1)}, f32[1,6,128]{2,0,1:T(1,128)}, u32[]{:S(2)}) copy-start(f32[1,6,128]{2,0,1:T(1,128)} %param.13) | copy-start | bytes 9220
  167.2 6.3 %collective-permute-start.3 = (f32[7,128]{1,0:T(8,128)S(1)}, f32[7,128]{1,0:T(8,128)S(1)}, u32[]{:S(2)}, u32[]{:S(2)}) collective-permute-start(f32[7,128]{1,0:T(8,128)S(1)} %concatenate.93), channel_id=1, source_target_pairs={{1,0},{2,1},{3,2},{4,3},{5,4},{6,5},{7,6},{9,8},{10,9},{11,10},{12... | collective-permute-start | bytes 10760 | tf_op jit(solution)/shard_map/ppermute | solution.py:30
  168.5 6.3 %collective-permute-start.2 = (f32[7,128]{1,0:T(8,128)S(1)}, f32[7,128]{1,0:T(8,128)S(1)}, u32[]{:S(2)}, u32[]{:S(2)}) collective-permute-start(f32[7,128]{1,0:T(8,128)S(1)} %concatenate.93), channel_id=1, source_target_pairs={{0,1},{1,2},{2,3},{3,4},{4,5},{5,6},{6,7},{8,9},{9,10},{10,11},{11... | collective-permute-start | bytes 10760 | tf_op jit(solution)/shard_map/ppermute | solution.py:29
  197.0 11.9 %copy-start.1 = (f32[3,16,152,128]{3,2,1,0:T(8,128)S(1)}, f32[3,16,152,128]{3,2,1,0:T(8,128)}, u32[]{:S(2)}) copy-start(f32[3,16,152,128]{3,2,1,0:T(8,128)} %copy-done) | copy-start | bytes 11206660
  208.9 6.2 %copy-start.14 = (f32[16,152,128]{2,1,0:T(8,128)}, f32[16,152,128]{2,1,0:T(8,128)S(1)}, u32[]{:S(2)}) copy-start(f32[16,152,128]{2,1,0:T(8,128)S(1)} %get-tuple-element.23) | copy-start | bytes 3735556
  208.9 6.2 %copy-start.20 = (f32[16,152,128]{2,1,0:T(8,128)}, f32[16,152,128]{2,1,0:T(8,128)S(1)}, u32[]{:S(2)}) copy-start(f32[16,152,128]{2,1,0:T(8,128)S(1)} %get-tuple-element.22) | copy-start | bytes 3735556
  238.6 5.9 %copy-start.25 = (f32[16,152,128]{2,1,0:T(8,128)S(1)}, f32[16,152,128]{2,1,0:T(8,128)}, u32[]{:S(2)}) copy-start(f32[16,152,128]{2,1,0:T(8,128)} %copy-done.24) | copy-start | bytes 3735556
  238.6 5.9 %copy-start.28 = (f32[16,152,128]{2,1,0:T(8,128)S(1)}, f32[16,152,128]{2,1,0:T(8,128)}, u32[]{:S(2)}) copy-start(f32[16,152,128]{2,1,0:T(8,128)} %get-tuple-element.28) | copy-start | bytes 3735556
  238.6 5.9 %copy-start.32 = (f32[16,152,128]{2,1,0:T(8,128)S(1)}, f32[16,152,128]{2,1,0:T(8,128)}, u32[]{:S(2)}) copy-start(f32[16,152,128]{2,1,0:T(8,128)} %copy-done.31) | copy-start | bytes 3735556
  238.6 5.9 %copy-start.37 = (f32[16,152,128]{2,1,0:T(8,128)S(1)}, f32[16,152,128]{2,1,0:T(8,128)}, u32[]{:S(2)}) copy-start(f32[16,152,128]{2,1,0:T(8,128)} %copy-done.36) | copy-start | bytes 3735556
  238.7 5.9 %copy-start.38 = (f32[16,152,128]{2,1,0:T(8,128)S(1)}, f32[16,152,128]{2,1,0:T(8,128)}, u32[]{:S(2)}) copy-start(f32[16,152,128]{2,1,0:T(8,128)} %get-tuple-element.8) | copy-start | bytes 3735556
  238.7 5.9 %copy-start.39 = (f32[16,152,128]{2,1,0:T(8,128)S(1)}, f32[16,152,128]{2,1,0:T(8,128)}, u32[]{:S(2)}) copy-start(f32[16,152,128]{2,1,0:T(8,128)} %get-tuple-element.25) | copy-start | bytes 3735556
  246.7 5.8 %copy-start.27 = (f32[16,152,128]{2,1,0:T(8,128)S(1)}, f32[16,152,128]{2,1,0:T(8,128)}, u32[]{:S(2)}) copy-start(f32[16,152,128]{2,1,0:T(8,128)} %get-tuple-element.29) | copy-start | bytes 3735556
  246.7 6.2 %copy-start.30 = (f32[16,152,128]{2,1,0:T(8,128)S(1)}, f32[16,152,128]{2,1,0:T(8,128)}, u32[]{:S(2)}) copy-start(f32[16,152,128]{2,1,0:T(8,128)} %copy-done.29) | copy-start | bytes 3735556
  246.7 6.5 %copy-start.35 = (f32[16,152,128]{2,1,0:T(8,128)S(1)}, f32[16,152,128]{2,1,0:T(8,128)}, u32[]{:S(2)}) copy-start(f32[16,152,128]{2,1,0:T(8,128)} %copy-done.34) | copy-start | bytes 3735556
  269.8 38.2 %copy-start.52 = (f32[3,4,128,128]{3,2,1,0:T(8,128)S(1)}, f32[3,4,128,128]{3,2,1,0:T(8,128)}, u32[]{:S(2)}) copy-start(f32[3,4,128,128]{3,2,1,0:T(8,128)} %param.7) | copy-start | bytes 2359300
  (37 other events, 122.5 us)
Sparse Core Ops, SparseCore 0:
  9.5 31.2 all-gather.1
  267.0 40.9 reduce-scatter.1
where the time goes:
time: 322 us; the launch traced here: 317 us
  other arithmetic  163 us (51%)
  waiting for transfers between devices  64.1 us (20%)
  local copies, waits for them, and re-layouts  44.4 us (14%)
  starting transfers between devices  20.7 us (6%)
  between operations  17.5 us (5%)
  blocking collectives  7.56 us (2%)
    reduce_scatter x1, waiting for transfers between devices, per_device(): summed = lax.psum_scatter(acc, 'shot', scatter_dimension=0, tiled=True)[0]  36.7 us
    add x6, other arithmetic, per_device(): 2.0 * upper - upper_old + speed * (stretch * h + couple * z) + pulse  29.4 us
    scatter-add x6, other arithmetic, per_device(): inject = jnp.zeros((cells_ext,), jnp.float32).at[rec_all].add(vals, mode=...  26.7 us
    add x4, other arithmetic, per_device(): lower_next = 2.0 * lower - lower_old + speed * (couple * h + z) + pulse  24.6 us
    mul x5, other arithmetic, per_device(): first = speed * (stretch * lam + couple * mu)  23.8 us
    unnamed x122, local copies, waits for them, and re-layouts  20.3 us
    ppermute x3, waiting for transfers between devices, to_left_right(): from_left = lax.ppermute(tail, axis, [(i, i + 1) for i in range(count - 1)])  20 us
    ppermute x3, starting transfers between devices, to_left_right(): from_left = lax.ppermute(tail, axis, [(i, i + 1) for i in range(count - 1)])  16.7 us
  transfers between devices with their start and end apart: 8, of which 4 were waited for; matrix products, arithmetic and copies ran while one was open for 9% of the time, Pallas kernels for 0%

commit v1 on v0

--- a/solution.py
+++ b/solution.py
@@ -4,6 +4,23 @@
 from jax.sharding import PartitionSpec as P
 
 HALO = 12
+
+
+def in_order(blocks, dim):
+    blocks = jnp.moveaxis(blocks, 0, dim)
+    shape = blocks.shape
+    return blocks.reshape(*shape[:dim], shape[dim] * shape[dim + 1], *shape[dim + 2 :])
+
+
+def gather_around(value, axis, dim):
+    size = lax.axis_size(axis)
+    right = [(i, (i + 1) % size) for i in range(size)]
+    blocks = [value]
+    while len(blocks) < size:
+        blocks.append(lax.ppermute(blocks[-1], axis, right))
+    index = lax.axis_index(axis)
+    blocks = jnp.stack(blocks)[(index - jnp.arange(size)) % size]
+    return in_order(blocks, dim)
 
 
 def taps(padded, size, axis):
@@ -64,7 +81,7 @@
 
     st_l, cf_l, sc_l = unpack1(left1)
     st_r, cf_r, sc_r = unpack1(right1)
-    cf_halo = lax.all_gather(jnp.concatenate([cf_l, cf_r], axis=2), "shot", axis=1, tiled=True)
+    cf_halo = gather_around(jnp.concatenate([cf_l, cf_r], axis=2), "shot", 1)
     full_ext = jnp.concatenate([cf_halo[:, :, :w], full, cf_halo[:, :, w:]], axis=2)
     speed, stretch, couple = (full_ext[0], full_ext[1], full_ext[2])
     state = jnp.concatenate([st_l, fs, st_r], axis=2)

time: 322 us -> 327 us (1.016)
  local copies, waits for them, and re-layouts: 44.4 us -> 52.5 us
  blocking collectives: 7.56 us -> 0 us
    all_gather x1 -> x0, blocking collectives: 7.56 us -> none  [per_device(): lax.all_gather(jnp.concatenate([cf_l, cf_r], axis=2), 'shot', axis=1, til...]
    reshape x2, local copies, waits for them, and re-layouts: 0.07 us -> 3.65 us  [unpack1(): st = m[:n_fs].reshape(4, az, w, ay)]
    unnamed x122 -> x124, local copies, waits for them, and re-layouts: 20.3 us -> 18.3 us
  transfers between devices with their start and end apart: 8 -> 11, of which waited for: 4 -> 5; matrix products, arithmetic and copies ran while one was open for 9% -> 13% of each run, Pallas kernels for 0% -> 0%
where the time goes in v1:
time: 327 us; the launch traced here: 322 us
  other arithmetic  163 us (50%)
  waiting for transfers between devices  66.9 us (20%)
  local copies, waits for them, and re-layouts  52.5 us (16%)
  starting transfers between devices  22.1 us (7%)
  between operations  17.5 us (5%)
    reduce_scatter x1, waiting for transfers between devices, per_device(): summed = lax.psum_scatter(acc, 'shot', scatter_dimension=0, tiled=True)[0]  36 us
    add x6, other arithmetic, per_device(): 2.0 * upper - upper_old + speed * (stretch * h + couple * z) + pulse  29.2 us
    scatter-add x6, other arithmetic, per_device(): inject = jnp.zeros((cells_ext,), jnp.float32).at[rec_all].add(vals, mode=...  26.7 us
    add x4, other arithmetic, per_device(): lower_next = 2.0 * lower - lower_old + speed * (couple * h + z) + pulse  24.9 us
    mul x5, other arithmetic, per_device(): first = speed * (stretch * lam + couple * mu)  23.4 us
    ppermute x3, waiting for transfers between devices, to_left_right(): from_left = lax.ppermute(tail, axis, [(i, i + 1) for i in range(count - 1)])  19.9 us
    unnamed x124, local copies, waits for them, and re-layouts  18.3 us
    ppermute x3, starting transfers between devices, to_left_right(): from_left = lax.ppermute(tail, axis, [(i, i + 1) for i in range(count - 1)])  16 us
  transfers between devices with their start and end apart: 11, of which 5 were waited for; matrix products, arithmetic and copies ran while one was open for 13% of the time, Pallas kernels for 0%

profile of v1, /device:TPU:0, one launch (start us, length us, event | category | flops | bytes accessed | tf_op | source)
XLA Modules:
  0.0 322.5 jit_solution(4403478236334659430)
XLA Ops:
  12.6 6.3 %collective-permute-start = (f32[913,128]{1,0:T(8,128)S(1)}, f32[913,128]{1,0:T(8,128)}, u32[]{:S(2)}, u32[]{:S(2)}) collective-permute-start(f32[913,128]{1,0:T(8,128)S(1)} %get-tuple-element.91), channel_id=1, source_target_pairs={{0,1},{1,2},{2,3},{3,4},{4,5},{5,6},{6,7},{8,9},{9,10},{10,11},{11... | collective-permute-start | bytes 1402376 | tf_op jit(solution)/shard_map/ppermute | solution.py:46
  21.7 4.7 %collective-permute-start.7 = (f32[768,128]{1,0:T(8,128)S(1)}, f32[768,128]{1,0:T(8,128)S(1)}, u32[]{:S(2)}, u32[]{:S(2)}) collective-permute-start(f32[768,128]{1,0:T(8,128)S(1)} %reshape.684), channel_id=1, source_target_pairs={{0,1},{1,2},{2,3},{3,4},{4,5},{5,6},{6,7},{8,9},{9,10},{10,11},{11... | collective-permute-start | bytes 1179656 | tf_op jit(solution)/shard_map/ppermute | solution.py:46
  27.2 8.1 %collective-permute-done.8 = f32[768,128]{1,0:T(8,128)S(1)} collective-permute-done((f32[768,128]{1,0:T(8,128)S(1)}, f32[768,128]{1,0:T(8,128)S(1)}, u32[]{:S(2)}, u32[]{:S(2)}) %collective-permute-start.8) | collective-permute-done | bytes 393248 | tf_op jit(solution)/shard_map/ppermute | solution.py:47
  35.4 18.6 %collective-permute-done.7 = f32[768,128]{1,0:T(8,128)S(1)} collective-permute-done((f32[768,128]{1,0:T(8,128)S(1)}, f32[768,128]{1,0:T(8,128)S(1)}, u32[]{:S(2)}, u32[]{:S(2)}) %collective-permute-start.7) | collective-permute-done | bytes 393248 | tf_op jit(solution)/shard_map/ppermute | solution.py:46
  62.3 7.3 %broadcast_multiply_fusion = (f32[311296]{0:T(1024)}, f32[311296]{0:T(1024)}, f32[311296]{0:T(1024)}, f32[311296]{0:T(1024)}, f32[311296]{0:T(1024)S(1)}, /*index=5*/f32[311296]{0:T(1024)S(1)}) fusion(f32[311296]{0:T(1024)} %scatter_custom_fusion, f32[]{:T(128)} %bitcast.53, f32[]{:T(128)} %bitcast.48, f32[]{:T(128)} %bitcast.43, f32[]{:T(128)} %bitcast.38, ...), kind=kLoop, calls=%fused_computation.423 | loop fusion | flops 1867776 | bytes 8716312 | tf_op jit(solution)/shard_map/mul | solution.py:119
  78.7 5.9 %pad_maximum_fusion = (f32[4,16,152,128]{3,2,1,0:T(8,128)S(1)}, f32[4,16,152,128]{3,2,1,0:T(8,128)}) fusion(f32[4,16,12,128]{3,2,1,0:T(8,128)} %reshape.673, f32[4,16,128,128]{3,2,1,0:T(8,128)} %bitcast.475, f32[4,16,12,128]{3,2,1,0:T(8,128)} %reshape.670, f32[4,16,12,128]{3,2,1,0:T(8,128)S(1)} %reshape.687, f32[4,16,128,128]{3,2,1,0:T(8,128)} %bitcast.477, ...), kind=kLoop, calls=%fused_computation.14 | loop fusion | flops 4980736 | bytes 19922944 | tf_op jit(solution)/shard_map/concatenate | solution.py:87
  93.2 2.3 pad_maximum_fusion.2
  99.4 5.0 %add_multiply_fusion.10 = (f32[16,152,128]{2,1,0:T(8,128)}, f32[16,152,128]{2,1,0:T(8,128)}, f32[16,152,128]{2,1,0:T(8,128)S(1)}, f32[16,152,128]{2,1,0:T(8,128)S(1)}, f32[16,152,128]{2,1,0:T(8,128)S(1)}) fusion(f32[4,16,152,128]{3,2,1,0:T(8,128)} %get-tuple-element.112, f32[3,16,152,128]{3,2,1,0:T(8,128)S(1)} %pad_maximum_fusion.2, ...), kind=kLoop, calls=%fused_computation.368 | loop fusion | flops 12451840 | bytes 18677760 | tf_op jit(solution)/shard_map/mul | solution.py:140
  110.5 3.0 add_add_fusion.5
  114.8 6.5 %add_add_fusion.3 = (f32[16,152,128]{2,1,0:T(8,128)}, f32[16,152,128]{2,1,0:T(8,128)}, f32[16,152,128]{2,1,0:T(8,128)}) fusion(f32[16,152,128]{2,1,0:T(8,128)S(1)} %bitcast.460, f32[16,152,128]{2,1,0:T(8,128)S(1)} %get-tuple-element.36, f32[16,152,128]{2,1,0:T(8,128)S(1)} %bitcast.442, f32[16,152,128]{2,1,0:T(8,128)S(1)} %get-tuple-element.35, ...), kind=kLoop, calls=%fused_computation.377 | loop fusion | flops 12451840 | bytes 16187392 | tf_op jit(solution)/shard_map/add | solution.py:121
  121.3 4.4 %add_add_fusion.4 = f32[16,152,128]{2,1,0:T(8,128)} fusion(f32[16,152,128]{2,1,0:T(8,128)} %bitcast.456, f32[16,152,128]{2,1,0:T(8,128)} %get-tuple-element.32, f32[16,152,128]{2,1,0:T(8,128)} %get-tuple-element.31, f32[3,16,152,128]{3,2,1,0:T(8,128)S(1)} %pad_maximum_fusion.2, f32[16,152,128]{2,1,0:T(8,128)S(1)} %bitcast.443, ...), kind=kLoop, calls=%fused_computation.380 | loop fusion | flops 7471104 | bytes 18677760 | tf_op jit(solution)/shard_map/add | solution.py:120
  125.7 13.1 %add_add_fusion.1 = (f32[16,152,128]{2,1,0:T(8,128)}, f32[16,152,128]{2,1,0:T(8,128)}, f32[16,152,128]{2,1,0:T(8,128)}) fusion(f32[16,152,128]{2,1,0:T(8,128)} %bitcast.461, f32[16,152,128]{2,1,0:T(8,128)} %bitcast.457, f32[16,152,128]{2,1,0:T(8,128)} %get-tuple-element.32, f32[16,152,128]{2,1,0:T(8,128)} %get-tuple-element.31, ...), kind=kLoop, calls=%fused_computation.373 | loop fusion | flops 14630912 | bytes 19922944 | tf_op jit(solution)/shard_map/add | solution.py:121
  138.8 6.9 %add_add_fusion.2 = f32[16,152,128]{2,1,0:T(8,128)} fusion(f32[16,152,128]{2,1,0:T(8,128)} %bitcast.462, f32[16,152,128]{2,1,0:T(8,128)} %get-tuple-element.29, f32[16,152,128]{2,1,0:T(8,128)} %get-tuple-element.28, f32[3,16,152,128]{3,2,1,0:T(8,128)S(1)} %pad_maximum_fusion.2, f32[16,152,128]{2,1,0:T(8,128)} %bitcast.458, ...), kind=kLoop, calls=%fused_computation.376 | loop fusion | flops 9961472 | bytes 22413312 | tf_op jit(solution)/shard_map/add | solution.py:120
  145.7 15.8 %add_add_fusion = (f32[16,152,128]{2,1,0:T(8,128)}, f32[16,152,128]{2,1,0:T(8,128)}, f32[16,152,128]{2,1,0:T(8,128)}) fusion(f32[16,152,128]{2,1,0:T(8,128)} %bitcast.466, f32[16,152,128]{2,1,0:T(8,128)} %bitcast.463, f32[16,152,128]{2,1,0:T(8,128)} %get-tuple-element.29, f32[16,152,128]{2,1,0:T(8,128)} %get-tuple-element.28, ...), kind=kLoop, calls=%fused_computation.372 | loop fusion | flops 20545536 | bytes 28639232 | tf_op jit(solution)/shard_map/add | solution.py:120
  174.9 5.0 %collective-permute-start.5 = (f32[7,128]{1,0:T(8,128)S(1)}, f32[7,128]{1,0:T(8,128)S(1)}, u32[]{:S(2)}, u32[]{:S(2)}) collective-permute-start(f32[7,128]{1,0:T(8,128)S(1)} %concatenate.93), channel_id=1, source_target_pairs={{0,1},{1,2},{2,3},{3,4},{4,5},{5,6},{6,7},{8,9},{9,10},{10,11},{11... | collective-permute-start | bytes 10760 | tf_op jit(solution)/shard_map/ppermute | solution.py:46
  181.3 4.4 %scatter_custom_fusion.1 = f32[311296]{0:T(1024)} fusion(s32[384]{0:T(512)S(1)} %fusion.260, f32[384]{0:T(512)S(1)} %pad_maximum_fusion.6, f32[]{:T(128)} %constant.242.clone.1), kind=kCustom, calls=%fused_computation.440 | custom fusion | flops 384 | bytes 1245188 | tf_op jit(solution)/shard_map/scatter-add | solution.py:145
  185.7 4.3 %scatter_custom_fusion.2 = f32[311296]{0:T(1024)} fusion(s32[384]{0:T(512)S(1)} %fusion.260, f32[384]{0:T(512)S(1)} %pad_maximum_fusion.7, f32[]{:T(128)} %constant.242.clone.1), kind=kCustom, calls=%fused_computation.438 | custom fusion | flops 384 | bytes 1245188 | tf_op jit(solution)/shard_map/scatter-add | solution.py:145
  190.0 4.4 %scatter_custom_fusion.3 = f32[311296]{0:T(1024)} fusion(s32[384]{0:T(512)S(1)} %fusion.260, f32[384]{0:T(512)S(1)} %pad_maximum_fusion.8, f32[]{:T(128)} %constant.242.clone.1), kind=kCustom, calls=%fused_computation.436 | custom fusion | flops 384 | bytes 1245188 | tf_op jit(solution)/shard_map/scatter-add | solution.py:145
  194.4 4.4 %scatter_custom_fusion.4 = f32[311296]{0:T(1024)} fusion(s32[384]{0:T(512)S(1)} %fusion.260, f32[384]{0:T(512)S(1)} %pad_maximum_fusion.9, f32[]{:T(128)} %constant.242.clone.1), kind=kCustom, calls=%fused_computation.434 | custom fusion | flops 384 | bytes 1245188 | tf_op jit(solution)/shard_map/scatter-add | solution.py:145
  198.8 4.6 %scatter_custom_fusion.5 = f32[311296]{0:T(1024)} fusion(s32[384]{0:T(512)S(1)} %fusion.260, f32[384]{0:T(512)S(1)} %pad_maximum_fusion.10, f32[]{:T(128)} %constant.242.clone.1), kind=kCustom, calls=%fused_computation.432 | custom fusion | flops 384 | bytes 1245188 | tf_op jit(solution)/shard_map/scatter-add | solution.py:145
  203.4 11.5 %add_multiply_fusion.9 = (f32[16,152,128]{2,1,0:T(8,128)S(1)}, f32[16,152,128]{2,1,0:T(8,128)S(1)}, f32[16,152,128]{2,1,0:T(8,128)S(1)}) fusion(f32[3,16,152,128]{3,2,1,0:T(8,128)} %copy-done, f32[4,16,152,128]{3,2,1,0:T(8,128)} %get-tuple-element.112, f32[16,152,128]{2,1,0:T(8,128)} %get-tuple-element.43, f32[16,152,128]{2,1,0:T(8,128)} %bitcast.483, ...), kind=kLoop, calls=%fused_computation.367 | loop fusion | flops 11517952 | bytes 16187392 | tf_op jit(solution)/shard_map/mul | solution.py:139
  217.1 3.7 %add_multiply_fusion.7 = (f32[16,152,128]{2,1,0:T(8,128)S(1)}, f32[16,152,128]{2,1,0:T(8,128)S(1)}, f32[16,152,128]{2,1,0:T(8,128)S(1)}) fusion(f32[3,16,152,128]{3,2,1,0:T(8,128)S(1)} %copy-done.1, f32[4,16,152,128]{3,2,1,0:T(8,128)} %get-tuple-element.112, f32[16,152,128]{2,1,0:T(8,128)S(1)} %get-tuple-element.21, f32[16,152,128]{2,1,0:T(8,128)S(1)} %bitcast.482, ...), kind=kLoop, calls=%fused_computation.363 | loop fusion | flops 11517952 | bytes 16187392 | tf_op jit(solution)/shard_map/mul | solution.py:139
  223.1 2.4 add_multiply_fusion.5
  227.7 2.4 add_multiply_fusion.3
  232.3 3.4 %add_multiply_fusion.1 = (f32[16,152,128]{2,1,0:T(8,128)S(1)}, f32[16,152,128]{2,1,0:T(8,128)}, f32[16,152,128]{2,1,0:T(8,128)}) fusion(f32[3,16,152,128]{3,2,1,0:T(8,128)S(1)} %copy-done.1, f32[16,152,128]{2,1,0:T(8,128)S(1)} %get-tuple-element.16, f32[16,152,128]{2,1,0:T(8,128)S(1)} %get-tuple-element.12, f32[16,152,128]{2,1,0:T(8,128)S(1)} %bitcast.479, ...), kind=kLoop, calls=%fused_computation.351 | loop fusion | flops 11517952 | bytes 16187392 | tf_op jit(solution)/shard_map/mul | solution.py:139
  235.7 4.2 %add_subtract_fusion = (f32[16,152,128]{2,1,0:T(8,128)}, f32[16,152,128]{2,1,0:T(8,128)}, f32[16,152,128]{2,1,0:T(8,128)}, f32[16,152,128]{2,1,0:T(8,128)}, f32[16,152,128]{2,1,0:T(8,128)}, /*index=5*/f32[16,152,128]{2,1,0:T(8,128)}) fusion(f32[16,152,128]{2,1,0:T(8,128)S(1)} %get-tuple-element.7), kind=kLoop, calls=%fused_computation.350 | loop fusion | flops 3424256 | bytes 8716288 | tf_op jit(solution)/shard_map/sub | solution.py:31
  239.9 4.7 %scatter_custom_fusion.6 = f32[311296]{0:T(1024)} fusion(s32[384]{0:T(512)S(1)} %fusion.260, f32[384]{0:T(512)S(1)} %pad_maximum_fusion.11, f32[]{:T(128)} %constant.242.clone.1), kind=kCustom, calls=%fused_computation.430 | custom fusion | flops 384 | bytes 1245188 | tf_op jit(solution)/shard_map/scatter-add | solution.py:145
  244.6 3.9 %broadcast_multiply_fusion.6 = (f32[16,152,128]{2,1,0:T(8,128)}, f32[16,152,128]{2,1,0:T(8,128)S(1)}) fusion(f32[16,152,128]{2,1,0:T(8,128)} %get-tuple-element.9, f32[16,152,128]{2,1,0:T(8,128)} %get-tuple-element.8, f32[3,16,152,128]{3,2,1,0:T(8,128)} %copy-done), kind=kLoop, calls=%fused_computation.429 | loop fusion | flops 1245184 | bytes 7471104 | tf_op jit(solution)/shard_map/mul | solution.py:31
  252.7 5.2 %multiply_add_fusion.2 = (f32[16,128,128]{2,1,0:T(8,128)}, f32[16,128,128]{2,1,0:T(8,128)S(1)}) fusion(f32[16,152,128]{2,1,0:T(8,128)S(1)} %copy-done.37, f32[16,152,128]{2,1,0:T(8,128)S(1)} %copy-done.7, f32[16,152,128]{2,1,0:T(8,128)S(1)} %get-tuple-element.34, f32[16,152,128]{2,1,0:T(8,128)S(1)} %copy-done.12, f32[16,152,128]{2,1,0:T(8,128)S(1)} %copy-done.25, ...), kind=kLoop, calls=%fused_computation.421 | loop fusion | flops 5505024 | bytes 20971520 | tf_op jit(solution)/shard_map/add | solution.py:153
  259.2 6.5 %multiply_add_fusion.1 = (f32[16,128,128]{2,1,0:T(8,128)}, f32[16,128,128]{2,1,0:T(8,128)}) fusion(f32[16,128,128]{2,1,0:T(8,128)S(1)} %get-tuple-element.4, f32[16,152,128]{2,1,0:T(8,128)S(1)} %copy-done.35, f32[16,152,128]{2,1,0:T(8,128)S(1)} %copy-done.5, f32[16,152,128]{2,1,0:T(8,128)S(1)} %get-tuple-element.35, f32[16,152,128]{2,1,0:T(8,128)S(1)} %copy-done.19, ...), kind=kLoop, calls=%fused_computation.420 | loop fusion | flops 8126464 | bytes 30408704 | tf_op jit(solution)/shard_map/add | solution.py:154
  265.7 5.0 %fusion.232 = (f32[1,16,128,128]{3,2,1,0:T(8,128)S(1)}, f32[16,128,128]{2,1,0:T(8,128)S(1)}) fusion(f32[16,152,128]{2,1,0:T(8,128)} %bitcast.467, f32[16,152,128]{2,1,0:T(8,128)} %get-tuple-element.51, f32[16,152,128]{2,1,0:T(8,128)} %get-tuple-element.30, f32[16,152,128]{2,1,0:T(8,128)} %get-tuple-element.27, f32[16,152,128]{2,1,0:T(8,128)} %get-tuple-element.50, ...), kind=kLoop, calls=%fused_computation.395 | loop fusion | flops 4718592 | bytes 20971520 | tf_op jit(solution)/shard_map/stack | solution.py:164
  277.2 36.0 %reduce-scatter.2.cloned.1.call-done = f32[1,3,4,128,128]{4,3,2,1,0:T(8,128)} async-done(((f32[4,3,4,128,128]{4,3,2,1,0:T(8,128)}), f32[1,3,4,128,128]{4,3,2,1,0:T(8,128)}) %reduce-scatter.2.cloned.1.call-update) | async-done | bytes 786448 | tf_op jit(solution)/shard_map/reduce_scatter | solution.py:160
  (219 shorter events, 81.2 us)
Async XLA Ops:
  7.2 86.1 %all-gather.2.cloned.1.call-start = ((), (), s32[]{:S(2)}) async-start(), calls=%async_computation.1 | async-start | bytes 3932160 | tf_op jit(solution)/shard_map/all_gather | solution.py:61
  7.9 305.3 %reduce-scatter.2.cloned.1.call-start = ((), (), s32[]{:S(2)}) async-start(), calls=%async_computation.2 | async-start | bytes 3932160 | tf_op jit(solution)/shard_map/reduce_scatter | solution.py:160
  11.3 42.8 %collective-permute-start.1 = (f32[913,128]{1,0:T(8,128)S(1)}, f32[913,128]{1,0:T(8,128)}, u32[]{:S(2)}, u32[]{:S(2)}) collective-permute-start(f32[913,128]{1,0:T(8,128)S(1)} %get-tuple-element.92), channel_id=1, source_target_pairs={{1,0},{2,1},{3,2},{4,3},{5,4},{6,5},{7,6},{9,8},{10,9},{11,10},{12... | collective-permute-start | bytes 1402376 | tf_op jit(solution)/shard_map/ppermute | solution.py:47
  12.6 43.4 %collective-permute-start = (f32[913,128]{1,0:T(8,128)S(1)}, f32[913,128]{1,0:T(8,128)}, u32[]{:S(2)}, u32[]{:S(2)}) collective-permute-start(f32[913,128]{1,0:T(8,128)S(1)} %get-tuple-element.91), channel_id=1, source_target_pairs={{0,1},{1,2},{2,3},{3,4},{4,5},{5,6},{6,7},{8,9},{9,10},{10,11},{11... | collective-permute-start | bytes 1402376 | tf_op jit(solution)/shard_map/ppermute | solution.py:46
  20.3 6.1 %copy-start.59 = (s32[1,128]{1,0:T(1,128)S(1)}, s32[1,128]{1,0:T(1,128)}, u32[]{:S(2)}) copy-start(s32[1,128]{1,0:T(1,128)} %param.12) | copy-start | bytes 1540
  20.3 6.3 %copy-start.57 = (f32[1,6]{1,0:T(1,128)S(1)}, f32[1,6]{1,0:T(1,128)}, u32[]{:S(2)}) copy-start(f32[1,6]{1,0:T(1,128)} %param.11) | copy-start | bytes 76
  20.3 15.0 %collective-permute-start.8 = (f32[768,128]{1,0:T(8,128)S(1)}, f32[768,128]{1,0:T(8,128)S(1)}, u32[]{:S(2)}, u32[]{:S(2)}) collective-permute-start(f32[768,128]{1,0:T(8,128)S(1)} %reshape.686), channel_id=1, source_target_pairs={{1,0},{2,1},{3,2},{4,3},{5,4},{6,5},{7,6},{9,8},{10,9},{11,10},{12... | collective-permute-start | bytes 1179656 | tf_op jit(solution)/shard_map/ppermute | solution.py:47
  21.7 32.3 %collective-permute-start.7 = (f32[768,128]{1,0:T(8,128)S(1)}, f32[768,128]{1,0:T(8,128)S(1)}, u32[]{:S(2)}, u32[]{:S(2)}) collective-permute-start(f32[768,128]{1,0:T(8,128)S(1)} %reshape.684), channel_id=1, source_target_pairs={{0,1},{1,2},{2,3},{3,4},{4,5},{5,6},{6,7},{8,9},{9,10},{10,11},{11... | collective-permute-start | bytes 1179656 | tf_op jit(solution)/shard_map/ppermute | solution.py:46
  60.5 16.6 %collective-permute-start.2 = (f32[3,4,24,128]{3,2,1,0:T(8,128)}, f32[3,4,24,128]{3,2,1,0:T(8,128)}, u32[]{:S(2)}, u32[]{:S(2)}) collective-permute-start(f32[3,4,24,128]{3,2,1,0:T(8,128)} %pad_maximum_fusion.5), channel_id=1, source_target_pairs={{0,8},{8,16},{16,24},{24,0},{1,9},{9,17},{17,25},{25,1},{2,10},{10... | collective-permute-start | bytes 442376 | tf_op jit(solution)/shard_map/ppermute | solution.py:20
  69.6 38.6 %copy-start.9 = (f32[311296]{0:T(1024)}, f32[311296]{0:T(1024)S(1)}, u32[]{:S(2)}) copy-start(f32[311296]{0:T(1024)S(1)} %get-tuple-element.73) | copy-start | bytes 3735556
  77.1 7.5 %collective-permute-start.3 = (f32[3,4,24,128]{3,2,1,0:T(8,128)}, f32[3,4,24,128]{3,2,1,0:T(8,128)S(1)}, u32[]{:S(2)}, u32[]{:S(2)}) collective-permute-start(f32[3,4,24,128]{3,2,1,0:T(8,128)} %collective-permute-done.2), channel_id=1, source_target_pairs={{0,8},{8,16},{16,24},{24,0},{1,9},{9,17},{17,25},{25,1},{2,10},{10... | collective-permute-start | bytes 442376 | tf_op jit(solution)/shard_map/ppermute | solution.py:20
  84.5 5.1 %collective-permute-start.4 = (f32[3,4,24,128]{3,2,1,0:T(8,128)S(1)}, f32[3,4,24,128]{3,2,1,0:T(8,128)S(1)}, u32[]{:S(2)}, u32[]{:S(2)}) collective-permute-start(f32[3,4,24,128]{3,2,1,0:T(8,128)S(1)} %collective-permute-done.3), channel_id=1, source_target_pairs={{0,8},{8,16},{16,24},{24,0},{1,9},{9,17},{17,25},{25,1},{2,10},{10... | collective-permute-start | bytes 442376 | tf_op jit(solution)/shard_map/ppermute | solution.py:20
  95.6 50.1 %copy-start = (f32[3,16,152,128]{3,2,1,0:T(8,128)}, f32[3,16,152,128]{3,2,1,0:T(8,128)S(1)}, u32[]{:S(2)}) copy-start(f32[3,16,152,128]{3,2,1,0:T(8,128)S(1)} %pad_maximum_fusion.2) | copy-start | bytes 11206660
  104.4 10.0 %copy-start.26 = (f32[16,152,128]{2,1,0:T(8,128)}, f32[16,152,128]{2,1,0:T(8,128)S(1)}, u32[]{:S(2)}) copy-start(f32[16,152,128]{2,1,0:T(8,128)S(1)} %get-tuple-element.52) | copy-start | bytes 3735556
  105.9 15.4 %copy-start.8 = (f32[16,152,128]{2,1,0:T(8,128)}, f32[16,152,128]{2,1,0:T(8,128)S(1)}, u32[]{:S(2)}) copy-start(f32[16,152,128]{2,1,0:T(8,128)S(1)} %fusion.220) | copy-start | bytes 3735556
  108.2 6.2 %copy-start.33 = (f32[16,152,128]{2,1,0:T(8,128)}, f32[16,152,128]{2,1,0:T(8,128)S(1)}, u32[]{:S(2)}) copy-start(f32[16,152,128]{2,1,0:T(8,128)S(1)} %get-tuple-element.36) | copy-start | bytes 3735556
  108.2 37.5 %copy-start.4 = (f32[16,152,128]{2,1,0:T(8,128)}, f32[16,152,128]{2,1,0:T(8,128)S(1)}, u32[]{:S(2)}) copy-start(f32[16,152,128]{2,1,0:T(8,128)S(1)} %get-tuple-element.38) | copy-start | bytes 3735556
  108.2 37.5 %copy-start.6 = (f32[16,152,128]{2,1,0:T(8,128)}, f32[16,152,128]{2,1,0:T(8,128)S(1)}, u32[]{:S(2)}) copy-start(f32[16,152,128]{2,1,0:T(8,128)S(1)} %get-tuple-element.37) | copy-start | bytes 3735556
  114.4 6.9 %copy-start.41 = (f32[16,152,128]{2,1,0:T(8,128)}, f32[16,152,128]{2,1,0:T(8,128)S(1)}, u32[]{:S(2)}) copy-start(f32[16,152,128]{2,1,0:T(8,128)S(1)} %add_add_fusion.6) | copy-start | bytes 3735556
  163.6 10.0 %copy-start.58 = (f32[1,6,128]{2,0,1:T(1,128)S(1)}, f32[1,6,128]{2,0,1:T(1,128)}, u32[]{:S(2)}) copy-start(f32[1,6,128]{2,0,1:T(1,128)} %param.13) | copy-start | bytes 9220
  173.6 6.3 %collective-permute-start.6 = (f32[7,128]{1,0:T(8,128)S(1)}, f32[7,128]{1,0:T(8,128)S(1)}, u32[]{:S(2)}, u32[]{:S(2)}) collective-permute-start(f32[7,128]{1,0:T(8,128)S(1)} %concatenate.93), channel_id=1, source_target_pairs={{1,0},{2,1},{3,2},{4,3},{5,4},{6,5},{7,6},{9,8},{10,9},{11,10},{12... | collective-permute-start | bytes 10760 | tf_op jit(solution)/shard_map/ppermute | solution.py:47
  174.9 6.3 %collective-permute-start.5 = (f32[7,128]{1,0:T(8,128)S(1)}, f32[7,128]{1,0:T(8,128)S(1)}, u32[]{:S(2)}, u32[]{:S(2)}) collective-permute-start(f32[7,128]{1,0:T(8,128)S(1)} %concatenate.93), channel_id=1, source_target_pairs={{0,1},{1,2},{2,3},{3,4},{4,5},{5,6},{6,7},{8,9},{9,10},{10,11},{11... | collective-permute-start | bytes 10760 | tf_op jit(solution)/shard_map/ppermute | solution.py:46
  203.4 11.6 %copy-start.1 = (f32[3,16,152,128]{3,2,1,0:T(8,128)S(1)}, f32[3,16,152,128]{3,2,1,0:T(8,128)}, u32[]{:S(2)}) copy-start(f32[3,16,152,128]{3,2,1,0:T(8,128)} %copy-done) | copy-start | bytes 11206660
  214.9 6.2 %copy-start.14 = (f32[16,152,128]{2,1,0:T(8,128)}, f32[16,152,128]{2,1,0:T(8,128)S(1)}, u32[]{:S(2)}) copy-start(f32[16,152,128]{2,1,0:T(8,128)S(1)} %get-tuple-element.23) | copy-start | bytes 3735556
  214.9 6.2 %copy-start.20 = (f32[16,152,128]{2,1,0:T(8,128)}, f32[16,152,128]{2,1,0:T(8,128)S(1)}, u32[]{:S(2)}) copy-start(f32[16,152,128]{2,1,0:T(8,128)S(1)} %get-tuple-element.22) | copy-start | bytes 3735556
  244.6 5.9 %copy-start.25 = (f32[16,152,128]{2,1,0:T(8,128)S(1)}, f32[16,152,128]{2,1,0:T(8,128)}, u32[]{:S(2)}) copy-start(f32[16,152,128]{2,1,0:T(8,128)} %copy-done.24) | copy-start | bytes 3735556
  244.6 5.9 %copy-start.28 = (f32[16,152,128]{2,1,0:T(8,128)S(1)}, f32[16,152,128]{2,1,0:T(8,128)}, u32[]{:S(2)}) copy-start(f32[16,152,128]{2,1,0:T(8,128)} %get-tuple-element.28) | copy-start | bytes 3735556
  244.6 5.9 %copy-start.32 = (f32[16,152,128]{2,1,0:T(8,128)S(1)}, f32[16,152,128]{2,1,0:T(8,128)}, u32[]{:S(2)}) copy-start(f32[16,152,128]{2,1,0:T(8,128)} %copy-done.31) | copy-start | bytes 3735556
  244.6 5.9 %copy-start.37 = (f32[16,152,128]{2,1,0:T(8,128)S(1)}, f32[16,152,128]{2,1,0:T(8,128)}, u32[]{:S(2)}) copy-start(f32[16,152,128]{2,1,0:T(8,128)} %copy-done.36) | copy-start | bytes 3735556
  252.7 6.2 %copy-start.30 = (f32[16,152,128]{2,1,0:T(8,128)S(1)}, f32[16,152,128]{2,1,0:T(8,128)}, u32[]{:S(2)}) copy-start(f32[16,152,128]{2,1,0:T(8,128)} %copy-done.29) | copy-start | bytes 3735556
  252.7 6.5 %copy-start.35 = (f32[16,152,128]{2,1,0:T(8,128)S(1)}, f32[16,152,128]{2,1,0:T(8,128)}, u32[]{:S(2)}) copy-start(f32[16,152,128]{2,1,0:T(8,128)} %copy-done.34) | copy-start | bytes 3735556
  275.7 37.5 %copy-start.52 = (f32[3,4,128,128]{3,2,1,0:T(8,128)S(1)}, f32[3,4,128,128]{3,2,1,0:T(8,128)}, u32[]{:S(2)}) copy-start(f32[3,4,128,128]{3,2,1,0:T(8,128)} %param.7) | copy-start | bytes 2359300
  (41 other events, 144.0 us)
Sparse Core Ops, SparseCore 0:
  9.5 31.2 all-gather.1
  272.9 40.2 reduce-scatter.1
